TPU v7x, 32 devices: a whole 2x2x4 slice. The times are simulated.
32 devices in a mesh: panel: 2 (over y), lat: 4 (over z), lon: 4 (over x, core).
Axes of the slice: x: 2, y: 2, z: 4, core: 2. Of those that a mesh axis runs over, the one named last changes fastest.
Arguments:
- state: float32 [2, 7, 2, 256, 512], P('panel', None, None, 'lat', 'lon'), may hold values from -4 to 4
- source_slot: int32 [2, 4, 4, 768], P('panel', 'lat', 'lon'), may hold values from 0 to 3071, as said below
- donor_cell: int32 [2, 4, 4, 192], P('panel', 'lat', 'lon'), may hold values from 0 to 8000
- donor_frac: float32 [2, 4, 4, 2, 192], P('panel', 'lat', 'lon'), may hold values from 0 to 1
- donor_turn: float32 [2, 4, 4, 192], P('panel', 'lat', 'lon'), may hold values from -3.140625 to 3.140625
Outputs:
- new_state: float32 [2, 7, 2, 256, 512], P('panel', None, None, 'lat', 'lon')
Inputs may be any that keep to these rules, and one draw needn't show every extreme that they name: `source_slot`: entries name a partner panel donation (a * 4 + b) * 192 + s. For a device on an edge of its panel, the rim entries that lie on that edge name the donations that fill them; over a panel's whole border every donation of the partner panel is named exactly once. Other entries are unused.
All inputs are finite; a program needn't handle non-finite values.
Results may differ from a plain program's by a relative error of at most 0.00002.
Values sent between devices are 32-bit elements; how exact they have to be, the bound alone decides.
No kernel may reach another device: no remote copies, remote signals or barrier semaphores. Data moves between devices by JAX's collectives and lax.ppermute only.
A program may use at most 64 MiB of HBM per device.

v0:
```python
import jax
import jax.numpy as jnp
from jax import lax
from jax.sharding import PartitionSpec as P

viscosity = 0.05
resistivity = 0.05
diffusivity = 0.05
buoyancy = 0.5
time_step = 0.25
HIGHEST = lax.Precision.HIGHEST


def partner_2(block, axis, apart):
    count = lax.axis_size(axis)
    route = []
    for low in range(count):
        high = low | 1 << apart
        if high != low and high < count:
            route += [(low, high), (high, low)]
    return lax.ppermute(block, axis, route)


def shift(value, axis, step):
    size = lax.axis_size(axis)
    if step > 0:
        route = [(i, i + 1) for i in range(size - 1)]
    else:
        route = [(i + 1, i) for i in range(size - 1)]
    return lax.ppermute(value, axis, route)


def rate(up, mid, down, left, right):
    vert = jnp.concatenate([up, mid, down], axis=2)
    horz = jnp.concatenate([left, mid, right], axis=3)
    height = mid.shape[2]
    width = mid.shape[3]

    def lat_at(k):
        return vert[:, :, 2 + k : 2 + k + height, :]

    def lon_at(k):
        return horz[:, :, :, 2 + k : 2 + k + width]

    middle = mid
    d_lat = (8.0 * (lat_at(1) - lat_at(-1)) - (lat_at(2) - lat_at(-2))) / 12.0
    d_lon = (8.0 * (lon_at(1) - lon_at(-1)) - (lon_at(2) - lon_at(-2))) / 12.0
    padded = jnp.pad(middle, ((0, 0), (1, 1), (0, 0), (0, 0)))
    lap = lat_at(1) + lat_at(-1) + lon_at(1) + lon_at(-1) - 4.0 * middle
    lap = lap + padded[:, 2:] + padded[:, :-2] - 2.0 * middle
    adv_u = middle[1:2] * d_lat + middle[2:3] * d_lon
    adv_b = middle[4:5] * d_lat + middle[5:6] * d_lon
    moment = -adv_u[0:3] + adv_b[3:6] + viscosity * lap[0:3]
    induct = adv_b[0:3] - adv_u[3:6] + resistivity * lap[3:6]
    heat = -adv_u[6:7] + diffusivity * lap[6:7]
    first = moment[0:1] + buoyancy * middle[6:7]
    return jnp.concatenate([first, moment[1:3], induct, heat], axis=0)


def rotate(values, turn):
    cosine = jnp.cos(turn)
    sine = jnp.sin(turn)
    parts = [
        values[0],
        cosine * values[1] - sine * values[2],
        sine * values[1] + cosine * values[2],
        values[3],
        cosine * values[4] - sine * values[5],
        sine * values[4] + cosine * values[5],
        values[6],
    ]
    return jnp.stack(parts)


def per_device(state, source_slot, donor_cell, donor_frac, donor_turn):
    comps = state.shape[1]
    levels = state.shape[2]
    rows = state.shape[3]
    cols = state.shape[4]
    cells = donor_cell[0, 0, 0]
    frac_t = donor_frac[0, 0, 0, 0]
    frac_p = donor_frac[0, 0, 0, 1]
    turn = donor_turn[0, 0, 0]
    slots = source_slot[0, 0, 0]
    lat_pos = lax.axis_index("lat")
    lon_pos = lax.axis_index("lon")
    lat_count = lax.axis_size("lat")
    lon_count = lax.axis_size("lon")
    on_top = lat_pos == 0
    on_bottom = lat_pos == lat_count - 1
    on_left = lon_pos == 0
    on_right = lon_pos == lon_count - 1
    row = cells // (cols - 1)
    col = cells % (cols - 1)
    col_ids = jnp.arange(cols, dtype=jnp.int32)[None, :]
    row_ids = jnp.arange(rows, dtype=jnp.int32)[None, :]
    weight_lon = jnp.where(col_ids == col[:, None], (1.0 - frac_p)[:, None], 0.0) + jnp.where(
        col_ids == col[:, None] + 1, frac_p[:, None], 0.0
    )
    weight_lat = jnp.where(row_ids == row[:, None], (1.0 - frac_t)[:, None], 0.0) + jnp.where(
        row_ids == row[:, None] + 1, frac_t[:, None], 0.0
    )
    band = 2 * cols
    side = 2 * rows
    lat_slots = jnp.where(on_top, slots[0:band], slots[band : 2 * band])
    lon_slots = jnp.where(on_left, slots[2 * band : 2 * band + side], slots[2 * band + side :])
    wanted = jnp.concatenate([lat_slots, lon_slots])
    total = lax.axis_size("lat") * lax.axis_size("lon") * cells.shape[0]
    pick = (jnp.arange(total, dtype=jnp.int32)[:, None] == wanted[None, :]).astype(jnp.float32)

    def donate(field):
        flat = field.reshape(comps * levels, rows, cols)
        along = jnp.einsum("kij,sj->kis", flat, weight_lon, precision=HIGHEST)
        value = jnp.sum(along * weight_lat.T[None], axis=1)
        return rotate(value.reshape(comps, levels, -1), turn).reshape(comps * levels, -1)

    def receive(given):
        whole = lax.all_gather(given, ("lat", "lon"), axis=1, tiled=True)
        partner = partner_2(whole, "panel", 0)
        return jnp.dot(partner, pick, precision=HIGHEST)

    def section(field):
        up = shift(field[:, :, rows - 2 :, :], "lat", 1)
        down = shift(field[:, :, :2, :], "lat", -1)
        left = shift(field[:, :, :, cols - 2 :], "lon", 1)
        right = shift(field[:, :, :, :2], "lon", -1)
        rim = receive(donate(field)).reshape(comps, levels, -1)
        rim_lat = rim[:, :, :band].reshape(comps, levels, 2, cols)
        rim_lon = jnp.transpose(rim[:, :, band:].reshape(comps, levels, 2, rows), (0, 1, 3, 2))
        up = jnp.where(on_top, rim_lat, up)
        down = jnp.where(on_bottom, rim_lat, down)
        left = jnp.where(on_left, rim_lon, left)
        right = jnp.where(on_right, rim_lon, right)
        return rate(up, field, down, left, right)

    field = state[0]
    section_one = field + time_step * section(field)
    second = section(section_one)
    new_field = 0.5 * field + 0.5 * (section_one + time_step * second)
    return new_field[None]


def solution(mesh):
    in_specs = (
        P("panel", None, None, "lat", "lon"),
        P("panel", "lat", "lon", None),
        P("panel", "lat", "lon", None),
        P("panel", "lat", "lon", None, None),
        P("panel", "lat", "lon", None),
    )
    out_specs = P("panel", None, None, "lat", "lon")
    return jax.shard_map(
        per_device, mesh=mesh, in_specs=in_specs, out_specs=out_specs, check_vma=False
    )
```

profile of v0, /device:TPU:1, one launch (start us, length us, event | category | flops | bytes accessed | tf_op | source)
XLA Modules:
  0.0 83.6 jit_solution(6090372736300227283)
XLA Ops:
  0.0 0.0 copy-start.2
  0.0 0.7 broadcast_remainder_fusion
  0.7 0.7 compare_reduce_fusion
  1.4 0.8 fusion.71
  2.2 2.1 %fusion.6 = f32[14,192]{1,0:T(8,128)S(1)} fusion(f32[14,64,128]{2,1,0:T(8,128)} %bitcast.119, f32[64,192]{1,0:T(8,128)S(1)} %select_add_fusion.3, f32[192]{0:T(256)S(1)} %bitcast.153, s32[192]{0:T(256)S(1)} %get-tuple-element.50, f32[192]{0:T(256)S(1)} %broadcast_subtract_fusion.1, s32[192]{0:T(256)S(1)} %get-tuple-element.49), kind=kOutput, calls=%fused_computation.9 | convolution fusion | flops 264705408 | bytes 521728 | tf_op jit(solution)/shard_map/kij,sj->kis/dot_general | solution.py:113
  4.3 0.0 copy-done.2
  4.3 0.1 fusion.72
  4.5 23.7 %all-gather = f32[16,192,14]{1,2,0:T(8,128)S(1)} all-gather(f32[1,192,14]{1,2,0:T(8,128)S(1)} %bitcast.145), channel_id=1, replica_groups=mesh['panel'=2,'lat'=4,'lon'=4] {'lat','lon'}, dimensions={0}, use_global_device_ids=true | all-gather | bytes 182784 | tf_op jit(solution)/shard_map/all_gather | solution.py:118
  28.1 0.0 copy-start
  28.1 0.1 copy.18
  28.3 0.1 reshape.364
  28.4 1.3 %collective-permute-start = (f32[14,3072]{1,0:T(8,128)S(1)}, f32[14,3072]{1,0:T(8,128)S(1)}, u32[]{:S(2)}, u32[]{:S(2)}) collective-permute-start(f32[14,3072]{1,0:T(8,128)S(1)} %bitcast.127), channel_id=1, source_target_pairs={{0,16},{16,0},{1,17},{17,1},{2,18},{18,2},{3,19},{19,3},{4,20},{20... | collective-permute-start | bytes 516104 | tf_op jit(solution)/shard_map/ppermute | solution.py:21
  29.7 0.0 copy-done
  29.7 0.2 fusion.68
  29.9 0.0 copy-start.1
  29.9 2.4 %collective-permute-start.3 = (f32[7,2,64,2]{3,2,1,0:T(8,128)S(1)}, f32[7,2,64,2]{3,2,1,0:T(8,128)S(1)}, u32[]{:S(2)}, u32[]{:S(2)}) collective-permute-start(f32[7,2,64,2]{3,2,1,0:T(8,128)S(1)} %get-tuple-element.36), channel_id=1, source_target_pairs={{1,0},{2,1},{3,2},{5,4},{6,5},{7,6},{9,8},{10,9},{11,10},{13,12},{... | collective-permute-start | bytes 21512 | tf_op jit(solution)/shard_map/ppermute | solution.py:30
  32.3 3.2 %collective-permute-start.4 = (f32[7,2,64,2]{3,2,1,0:T(8,128)S(1)}, f32[7,2,64,2]{3,2,1,0:T(8,128)S(1)}, u32[]{:S(2)}, u32[]{:S(2)}) collective-permute-start(f32[7,2,64,2]{3,2,1,0:T(8,128)S(1)} %get-tuple-element.35), channel_id=1, source_target_pairs={{0,1},{1,2},{2,3},{4,5},{5,6},{6,7},{8,9},{9,10},{10,11},{12,13},{... | collective-permute-start | bytes 21512 | tf_op jit(solution)/shard_map/ppermute | solution.py:30
  35.5 1.3 %collective-permute-start.1 = (f32[7,2,2,128]{3,2,1,0:T(2,128)S(1)}, f32[7,2,2,128]{3,2,1,0:T(2,128)S(1)}, u32[]{:S(2)}, u32[]{:S(2)}) collective-permute-start(f32[7,2,2,128]{3,2,1,0:T(2,128)S(1)} %get-tuple-element.38), channel_id=1, source_target_pairs={{4,0},{8,4},{12,8},{5,1},{9,5},{13,9},{6,2},{10,6},{14,10},{7,3},{... | collective-permute-start | bytes 43016 | tf_op jit(solution)/shard_map/ppermute | solution.py:30
  36.8 4.0 %collective-permute-start.2 = (f32[7,2,2,128]{3,2,1,0:T(2,128)S(1)}, f32[7,2,2,128]{3,2,1,0:T(2,128)S(1)}, u32[]{:S(2)}, u32[]{:S(2)}) collective-permute-start(f32[7,2,2,128]{3,2,1,0:T(2,128)S(1)} %get-tuple-element.37), channel_id=1, source_target_pairs={{0,4},{4,8},{8,12},{1,5},{5,9},{9,13},{2,6},{6,10},{10,14},{3,7},{... | collective-permute-start | bytes 43016 | tf_op jit(solution)/shard_map/ppermute | solution.py:30
  40.8 0.0 copy-done.1
  40.9 0.0 collective-permute-done
  40.9 1.5 %fusion.1 = f32[14,384]{1,0:T(8,128)S(1)} fusion(f32[14,3072]{1,0:T(8,128)S(1)} %collective-permute-done, s32[384]{0:T(512)S(1)} %pad_add_fusion), kind=kOutput, calls=%fused_computation.2 | convolution fusion | flops 199360512 | bytes 195072 | tf_op jit(solution)/shard_map/dot_general | solution.py:120
  42.4 0.1 reshape.358
  42.5 0.2 copy.19
  42.8 0.0 collective-permute-done.3
  42.8 0.0 collective-permute-done.4
  42.8 0.1 bitcast_select_fusion.2
  42.9 0.0 collective-permute-done.1
  43.0 0.0 collective-permute-done.2
  43.0 0.9 %multiply_add_fusion.2 = (f32[7,2,64,128]{3,2,1,0:T(8,128)S(1)}, f32[7,2,64,128]{3,2,1,0:T(8,128)S(1)}, f32[7,2,64,128]{3,2,1,0:T(8,128)S(1)}) fusion(f32[2,64,128]{2,1,0:T(8,128)S(1)} %get-tuple-element.30, f32[2,64,128]{2,1,0:T(8,128)S(1)} %get-tuple-element.31, f32[7,2,64,128]{3,2,1,0:T(8,128)S(1)} %bitcast.122, ...), kind=kLoop, calls=%fused_computation.74 | loop fusion | flops 2179072 | bytes 2009088 | tf_op jit(solution)/shard_map/add | solution.py:52
  43.9 0.6 fusion.17
  44.5 0.1 fusion.37
  44.7 0.1 maximum_multiply_fusion.1
  44.7 0.9 %fusion.66 = (f32[7,2,64,2]{3,2,1,0:T(8,128)S(1)}, f32[7,2,64,2]{3,2,1,0:T(8,128)}) fusion(f32[7,2,64,128]{3,2,1,0:T(8,128)S(1)} %get-tuple-element.28), kind=kLoop, calls=%fused_computation.175 | loop fusion | bytes 28672 | tf_op jit(solution)/shard_map/slice | solution.py:125
  45.7 1.0 %fusion.5 = f32[14,192]{1,0:T(8,128)S(1)} fusion(f32[14,64,128]{2,1,0:T(8,128)S(1)} %bitcast_add_fusion, f32[64,192]{1,0:T(8,128)S(1)} %select_add_fusion.3, f32[192]{0:T(256)S(1)} %bitcast.154, s32[192]{0:T(256)S(1)} %get-tuple-element.50, f32[192]{0:T(256)S(1)} %broadcast_subtract_fusion.1, s32[192]{0:T(256)S(1)} %get-tuple-element.49), kind=kOutput, calls=%fused_computation.8 | convolution fusion | flops 264705408 | bytes 521728 | tf_op jit(solution)/shard_map/kij,sj->kis/dot_general | solution.py:113
  46.9 18.7 %all-gather.1 = f32[16,192,14]{1,2,0:T(8,128)S(1)} all-gather(f32[1,192,14]{1,2,0:T(8,128)S(1)} %bitcast.146), channel_id=1, replica_groups=mesh['panel'=2,'lat'=4,'lon'=4] {'lat','lon'}, dimensions={0}, use_global_device_ids=true | all-gather | bytes 182784 | tf_op jit(solution)/shard_map/all_gather | solution.py:118
  65.6 0.1 copy.20
  65.7 0.1 reshape.366
  65.8 0.6 collective-permute-start.5
  66.5 2.3 %collective-permute-start.8 = (f32[7,2,64,2]{3,2,1,0:T(8,128)}, f32[7,2,64,2]{3,2,1,0:T(8,128)S(1)}, u32[]{:S(2)}, u32[]{:S(2)}) collective-permute-start(f32[7,2,64,2]{3,2,1,0:T(8,128)} %get-tuple-element.24), channel_id=1, source_target_pairs={{1,0},{2,1},{3,2},{5,4},{6,5},{7,6},{9,8},{10,9},{11,10},{13,12},{... | collective-permute-start | bytes 21512 | tf_op jit(solution)/shard_map/ppermute | solution.py:30
  68.8 3.2 %collective-permute-start.9 = (f32[7,2,64,2]{3,2,1,0:T(8,128)S(1)}, f32[7,2,64,2]{3,2,1,0:T(8,128)}, u32[]{:S(2)}, u32[]{:S(2)}) collective-permute-start(f32[7,2,64,2]{3,2,1,0:T(8,128)S(1)} %get-tuple-element.23), channel_id=1, source_target_pairs={{0,1},{1,2},{2,3},{4,5},{5,6},{6,7},{8,9},{9,10},{10,11},{12,13},{... | collective-permute-start | bytes 21512 | tf_op jit(solution)/shard_map/ppermute | solution.py:30
  72.1 1.3 %collective-permute-start.6 = (f32[7,2,2,128]{3,2,1,0:T(2,128)S(1)}, f32[7,2,2,128]{3,2,1,0:T(2,128)S(1)}, u32[]{:S(2)}, u32[]{:S(2)}) collective-permute-start(f32[7,2,2,128]{3,2,1,0:T(2,128)S(1)} %get-tuple-element.26), channel_id=1, source_target_pairs={{4,0},{8,4},{12,8},{5,1},{9,5},{13,9},{6,2},{10,6},{14,10},{7,3},{... | collective-permute-start | bytes 43016 | tf_op jit(solution)/shard_map/ppermute | solution.py:30
  73.4 4.6 %collective-permute-start.7 = (f32[7,2,2,128]{3,2,1,0:T(2,128)S(1)}, f32[7,2,2,128]{3,2,1,0:T(2,128)}, u32[]{:S(2)}, u32[]{:S(2)}) collective-permute-start(f32[7,2,2,128]{3,2,1,0:T(2,128)S(1)} %get-tuple-element.25), channel_id=1, source_target_pairs={{0,4},{4,8},{8,12},{1,5},{5,9},{9,13},{2,6},{6,10},{10,14},{3,7},{... | collective-permute-start | bytes 43016 | tf_op jit(solution)/shard_map/ppermute | solution.py:30
  78.0 0.0 collective-permute-done.5
  78.0 1.5 %fusion = f32[14,384]{1,0:T(8,128)S(1)} fusion(f32[14,3072]{1,0:T(8,128)S(1)} %collective-permute-done.5, s32[384]{0:T(512)S(1)} %pad_add_fusion), kind=kOutput, calls=%fused_computation.1 | convolution fusion | flops 199360512 | bytes 195072 | tf_op jit(solution)/shard_map/dot_general | solution.py:120
  79.5 0.1 reshape.362
  79.6 0.2 copy.21
  79.8 0.0 collective-permute-done.8
  79.8 0.0 collective-permute-done.9
  79.8 1.1 %bitcast_select_fusion = (f32[7,2,64,2]{3,2,1,0:T(8,128)S(1)}, f32[7,2,64,2]{3,2,1,0:T(8,128)S(1)}) fusion(f32[7,2,64,2]{3,2,1,0:T(8,128)} %collective-permute-done.9, f32[7,2,2,64]{2,3,1,0:T(8,128)S(1)} %copy.21, pred[]{:T(512)S(6)} %eq.104, f32[7,2,64,2]{3,2,1,0:T(8,128)S(1)} %collective-permute-done.8, pred[]{:T(512)S(6)} %eq.107), kind=kLoop, calls=%fused_computation.67 | loop fusion | flops 3584 | bytes 35842 | tf_op jit(solution)/shard_map/jit(_where)/select_n | solution.py:132
  81.0 0.0 collective-permute-done.6
  81.0 0.0 collective-permute-done.7
  81.1 0.5 fusion.20
  81.6 0.9 %multiply_add_fusion = (f32[7,2,64,128]{3,2,1,0:T(8,128)S(1)}, f32[7,2,64,128]{3,2,1,0:T(8,128)S(1)}, f32[7,2,64,128]{3,2,1,0:T(8,128)S(1)}) fusion(f32[2,64,128]{2,1,0:T(8,128)S(1)} %get-tuple-element.20, f32[2,64,128]{2,1,0:T(8,128)S(1)} %get-tuple-element.18, f32[7,2,64,128]{3,2,1,0:T(8,128)S(1)} %get-tuple-element.28, ...), kind=kLoop, calls=%fused_computation.72 | loop fusion | flops 2179072 | bytes 2009088 | tf_op jit(solution)/shard_map/add | solution.py:52
  82.5 0.1 multiply_add_fusion.1
  82.6 0.1 fusion.35
  82.7 0.9 %fusion.32 = f32[1,7,2,64,128]{4,3,2,1,0:T(8,128)} fusion(f32[1,7,2,64,128]{4,3,2,1,0:T(8,128)S(1)} %copy-done, f32[1,1,2,64,128]{4,3,2,1,0:T(8,128)S(1)} %bitcast.126, f32[1,3,2,64,128]{4,3,2,1,0:T(8,128)S(1)} %bitcast.124, f32[1,2,2,64,128]{4,3,2,1,0:T(8,128)S(1)} %get-tuple-element.40, f32[1,1,2,64,128]{4,3,2,1,0:T(8,128)S(1)} %bitcast.125, ...), kind=kLoop, calls=%fused_computation.64 | loop fusion | flops 1376256 | bytes 1835008 | tf_op jit(solution)/shard_map/add | solution.py:139
  (44 shorter events, 0.6 us)
Async XLA Ops:
  0.0 4.3 %copy-start.2 = (f32[1,1,1,192]{3,2,1,0:T(1,128)S(1)}, f32[1,1,1,192]{3,2,1,0:T(1,128)}, u32[]{:S(2)}) copy-start(f32[1,1,1,192]{3,2,1,0:T(1,128)} %param.9) | copy-start | bytes 2308
  28.1 1.6 %copy-start = (f32[1,7,2,64,128]{4,3,2,1,0:T(8,128)S(1)}, f32[1,7,2,64,128]{4,3,2,1,0:T(8,128)}, u32[]{:S(2)}) copy-start(f32[1,7,2,64,128]{4,3,2,1,0:T(8,128)} %param.5) | copy-start | bytes 1376260
  28.4 12.5 %collective-permute-start = (f32[14,3072]{1,0:T(8,128)S(1)}, f32[14,3072]{1,0:T(8,128)S(1)}, u32[]{:S(2)}, u32[]{:S(2)}) collective-permute-start(f32[14,3072]{1,0:T(8,128)S(1)} %bitcast.127), channel_id=1, source_target_pairs={{0,16},{16,0},{1,17},{17,1},{2,18},{18,2},{3,19},{19,3},{4,20},{20... | collective-permute-start | bytes 516104 | tf_op jit(solution)/shard_map/ppermute | solution.py:21
  29.9 11.0 %copy-start.1 = (s32[1,1,1,768]{3,2,1,0:T(1,128)S(1)}, s32[1,1,1,768]{3,2,1,0:T(1,128)}, u32[]{:S(2)}) copy-start(s32[1,1,1,768]{3,2,1,0:T(1,128)} %param.6) | copy-start | bytes 9220
  29.9 12.9 %collective-permute-start.3 = (f32[7,2,64,2]{3,2,1,0:T(8,128)S(1)}, f32[7,2,64,2]{3,2,1,0:T(8,128)S(1)}, u32[]{:S(2)}, u32[]{:S(2)}) collective-permute-start(f32[7,2,64,2]{3,2,1,0:T(8,128)S(1)} %get-tuple-element.36), channel_id=1, source_target_pairs={{1,0},{2,1},{3,2},{5,4},{6,5},{7,6},{9,8},{10,9},{11,10},{13,12},{... | collective-permute-start | bytes 21512 | tf_op jit(solution)/shard_map/ppermute | solution.py:30
  32.3 10.5 %collective-permute-start.4 = (f32[7,2,64,2]{3,2,1,0:T(8,128)S(1)}, f32[7,2,64,2]{3,2,1,0:T(8,128)S(1)}, u32[]{:S(2)}, u32[]{:S(2)}) collective-permute-start(f32[7,2,64,2]{3,2,1,0:T(8,128)S(1)} %get-tuple-element.35), channel_id=1, source_target_pairs={{0,1},{1,2},{2,3},{4,5},{5,6},{6,7},{8,9},{9,10},{10,11},{12,13},{... | collective-permute-start | bytes 21512 | tf_op jit(solution)/shard_map/ppermute | solution.py:30
  35.5 7.5 %collective-permute-start.1 = (f32[7,2,2,128]{3,2,1,0:T(2,128)S(1)}, f32[7,2,2,128]{3,2,1,0:T(2,128)S(1)}, u32[]{:S(2)}, u32[]{:S(2)}) collective-permute-start(f32[7,2,2,128]{3,2,1,0:T(2,128)S(1)} %get-tuple-element.38), channel_id=1, source_target_pairs={{4,0},{8,4},{12,8},{5,1},{9,5},{13,9},{6,2},{10,6},{14,10},{7,3},{... | collective-permute-start | bytes 43016 | tf_op jit(solution)/shard_map/ppermute | solution.py:30
  36.8 6.2 %collective-permute-start.2 = (f32[7,2,2,128]{3,2,1,0:T(2,128)S(1)}, f32[7,2,2,128]{3,2,1,0:T(2,128)S(1)}, u32[]{:S(2)}, u32[]{:S(2)}) collective-permute-start(f32[7,2,2,128]{3,2,1,0:T(2,128)S(1)} %get-tuple-element.37), channel_id=1, source_target_pairs={{0,4},{4,8},{8,12},{1,5},{5,9},{9,13},{2,6},{6,10},{10,14},{3,7},{... | collective-permute-start | bytes 43016 | tf_op jit(solution)/shard_map/ppermute | solution.py:30
  65.8 12.1 %collective-permute-start.5 = (f32[14,3072]{1,0:T(8,128)S(1)}, f32[14,3072]{1,0:T(8,128)S(1)}, u32[]{:S(2)}, u32[]{:S(2)}) collective-permute-start(f32[14,3072]{1,0:T(8,128)S(1)} %bitcast.128), channel_id=1, source_target_pairs={{0,16},{16,0},{1,17},{17,1},{2,18},{18,2},{3,19},{19,3},{4,20},{20... | collective-permute-start | bytes 516104 | tf_op jit(solution)/shard_map/ppermute | solution.py:21
  66.5 13.3 %collective-permute-start.8 = (f32[7,2,64,2]{3,2,1,0:T(8,128)}, f32[7,2,64,2]{3,2,1,0:T(8,128)S(1)}, u32[]{:S(2)}, u32[]{:S(2)}) collective-permute-start(f32[7,2,64,2]{3,2,1,0:T(8,128)} %get-tuple-element.24), channel_id=1, source_target_pairs={{1,0},{2,1},{3,2},{5,4},{6,5},{7,6},{9,8},{10,9},{11,10},{13,12},{... | collective-permute-start | bytes 21512 | tf_op jit(solution)/shard_map/ppermute | solution.py:30
  68.8 11.0 %collective-permute-start.9 = (f32[7,2,64,2]{3,2,1,0:T(8,128)S(1)}, f32[7,2,64,2]{3,2,1,0:T(8,128)}, u32[]{:S(2)}, u32[]{:S(2)}) collective-permute-start(f32[7,2,64,2]{3,2,1,0:T(8,128)S(1)} %get-tuple-element.23), channel_id=1, source_target_pairs={{0,1},{1,2},{2,3},{4,5},{5,6},{6,7},{8,9},{9,10},{10,11},{12,13},{... | collective-permute-start | bytes 21512 | tf_op jit(solution)/shard_map/ppermute | solution.py:30
  72.1 9.0 %collective-permute-start.6 = (f32[7,2,2,128]{3,2,1,0:T(2,128)S(1)}, f32[7,2,2,128]{3,2,1,0:T(2,128)S(1)}, u32[]{:S(2)}, u32[]{:S(2)}) collective-permute-start(f32[7,2,2,128]{3,2,1,0:T(2,128)S(1)} %get-tuple-element.26), channel_id=1, source_target_pairs={{4,0},{8,4},{12,8},{5,1},{9,5},{13,9},{6,2},{10,6},{14,10},{7,3},{... | collective-permute-start | bytes 43016 | tf_op jit(solution)/shard_map/ppermute | solution.py:30
  73.4 7.7 %collective-permute-start.7 = (f32[7,2,2,128]{3,2,1,0:T(2,128)S(1)}, f32[7,2,2,128]{3,2,1,0:T(2,128)}, u32[]{:S(2)}, u32[]{:S(2)}) collective-permute-start(f32[7,2,2,128]{3,2,1,0:T(2,128)S(1)} %get-tuple-element.25), channel_id=1, source_target_pairs={{0,4},{4,8},{8,12},{1,5},{5,9},{9,13},{2,6},{6,10},{10,14},{3,7},{... | collective-permute-start | bytes 43016 | tf_op jit(solution)/shard_map/ppermute | solution.py:30
where the time goes:
time: 84.2 us; the launch traced here: 83.6 us
  blocking collectives  42.4 us (50%)
  starting transfers between devices  24.2 us (29%)
  other arithmetic  7.14 us (8%)
  matrix products  6.06 us (7%)
  local copies, waits for them, and re-layouts  3.29 us (4%)
    all_gather x2, blocking collectives, receive(): whole = lax.all_gather(given, ('lat', 'lon'), axis=1, tiled=True)  42.4 us
    ppermute x8, starting transfers between devices, shift(): return lax.ppermute(value, axis, route)  22.3 us
    dot_general x2, matrix products, donate(): along = jnp.einsum('kij,sj->kis', flat, weight_lon, precision=HIGHEST)  3.09 us
    dot_general x2, matrix products, receive(): return jnp.dot(partner, pick, precision=HIGHEST)  2.97 us
    ppermute x2, starting transfers between devices, partner_2(): return lax.ppermute(block, axis, route)  1.94 us
    add x2, other arithmetic, rate(): adv_b = middle[4:5] * d_lat + middle[5:6] * d_lon  1.8 us
  transfers between devices with their start and end apart: 10, of which 0 were waited for; matrix products, arithmetic and copies ran while one was open for 6% of the time, Pallas kernels for 0%

commit v1 on v0

--- a/solution.py
+++ b/solution.py
@@ -115,7 +115,30 @@
         return rotate(value.reshape(comps, levels, -1), turn).reshape(comps * levels, -1)
 
     def receive(given):
-        whole = lax.all_gather(given, ("lat", "lon"), axis=1, tiled=True)
+        ways, here, step_2 = (
+            lax.axis_size(("lat", "lon")),
+            lax.axis_index(("lat", "lon")),
+            given.shape[1],
+        )
+        shape = [n * ways if d == 1 else n for d, n in enumerate(given.shape)]
+        whole = lax.dynamic_update_slice_in_dim(
+            jnp.zeros(shape, given.dtype), given, here * step_2, axis=1
+        )
+        going_up = going_down = given
+        for far in range(1, ways // 2 + 1):
+            going_up = lax.ppermute(
+                going_up, ("lat", "lon"), [(d, (d + 1) % ways) for d in range(ways)]
+            )
+            whole = lax.dynamic_update_slice_in_dim(
+                whole, going_up, (here - far) % ways * step_2, axis=1
+            )
+            if 2 * far < ways:
+                going_down = lax.ppermute(
+                    going_down, ("lat", "lon"), [(d, (d - 1) % ways) for d in range(ways)]
+                )
+                whole = lax.dynamic_update_slice_in_dim(
+                    whole, going_down, (here + far) % ways * step_2, axis=1
+                )
         partner = partner_2(whole, "panel", 0)
         return jnp.dot(partner, pick, precision=HIGHEST)
 

time: 84.2 us -> 138 us (1.64); the launches traced: 83.6 us -> 135 us
  starting transfers between devices: 24.2 us -> 90.7 us
  blocking collectives: 42.4 us -> 0 us
  waiting for transfers between devices: 0.03 us -> 15.2 us
  local copies, waits for them, and re-layouts: 3.29 us -> 14.6 us
    ppermute x0 -> x30, starting transfers between devices: none -> 60.5 us  [the longest x14 49.8 us: receive(): lax.ppermute(going_down, ('lat', 'lon'), [(d, (d - 1) % ways) for d in ra...]
    all_gather x2 -> x0, blocking collectives: 42.4 us -> none  [receive(): whole = lax.all_gather(given, ('lat', 'lon'), axis=1, tiled=True)]
    dynamic_update_slice x0 -> x32, local copies, waits for them, and re-layouts: none -> 12.6 us  [the longest x16 6.22 us: receive(): lax.dynamic_update_slice_in_dim(whole, going_up, (here - far) % ways * st...]
    ppermute x0 -> x30, waiting for transfers between devices: none -> 9.06 us  [the longest x16 7.19 us: receive(): lax.ppermute(going_up, ('lat', 'lon'), [(d, (d + 1) % ways) for d in rang...]
    ppermute x2, waiting for transfers between devices: 0.01 us -> 6.08 us  [partner_2(): return lax.ppermute(block, axis, route)]
    ppermute x8, starting transfers between devices: 22.3 us -> 26.6 us  [shift(): return lax.ppermute(value, axis, route)]
    ppermute x2, starting transfers between devices: 1.94 us -> 3.61 us  [partner_2(): return lax.ppermute(block, axis, route)]
  transfers between devices with their start and end apart: 10 -> 40, of which waited for: 0 -> 22; matrix products, arithmetic and copies ran while one was open for 6% -> 13% of each run, Pallas kernels for 0% -> 0%
where the time goes in v1:
time: 138 us; the launch traced here: 135 us
  starting transfers between devices  90.7 us (66%)
  waiting for transfers between devices  15.2 us (11%)
  local copies, waits for them, and re-layouts  14.6 us (11%)
  other arithmetic  7.91 us (6%)
  matrix products  6.06 us (4%)
    ppermute x14, starting transfers between devices, receive(): lax.ppermute(going_down, ('lat', 'lon'), [(d, (d - 1) % ways) for d in ra...  49.8 us
    ppermute x8, starting transfers between devices, shift(): return lax.ppermute(value, axis, route)  26.6 us
    ppermute x16, starting transfers between devices, receive(): lax.ppermute(going_up, ('lat', 'lon'), [(d, (d + 1) % ways) for d in rang...  10.7 us
    ppermute x16, waiting for transfers between devices, receive(): lax.ppermute(going_up, ('lat', 'lon'), [(d, (d + 1) % ways) for d in rang...  7.19 us
    dynamic_update_slice x16, local copies, waits for them, and re-layouts, receive(): lax.dynamic_update_slice_in_dim(whole, going_up, (here - far) % ways * st...  6.22 us
    ppermute x2, waiting for transfers between devices, partner_2(): return lax.ppermute(block, axis, route)  6.08 us
    dynamic_update_slice x14, local copies, waits for them, and re-layouts, receive(): lax.dynamic_update_slice_in_dim(whole, going_down, (here + far) % ways *...  5.42 us
    ppermute x2, starting transfers between devices, partner_2(): return lax.ppermute(block, axis, route)  3.61 us
  transfers between devices with their start and end apart: 40, of which 22 were waited for; matrix products, arithmetic and copies ran while one was open for 13% of the time, Pallas kernels for 0%

profile of v1, /device:TPU:1, one launch (start us, length us, event | category | flops | bytes accessed | tf_op | source)
XLA Modules:
  0.0 135.3 jit_solution(17869142375187274265)
XLA Ops:
  0.0 0.8 broadcast_remainder_fusion
  0.8 0.7 compare_reduce_fusion
  1.5 0.8 fusion.71
  2.3 2.1 %fusion.6 = f32[14,192]{1,0:T(8,128)S(1)} fusion(f32[14,64,128]{2,1,0:T(8,128)} %bitcast.107, f32[64,192]{1,0:T(8,128)S(1)} %select_add_fusion.3, f32[192]{0:T(256)S(1)} %bitcast.137, s32[192]{0:T(256)S(1)} %get-tuple-element.50, f32[192]{0:T(256)S(1)} %broadcast_subtract_fusion.1, s32[192]{0:T(256)S(1)} %get-tuple-element.49), kind=kOutput, calls=%fused_computation.9 | convolution fusion | flops 264705408 | bytes 521728 | tf_op jit(solution)/shard_map/kij,sj->kis/dot_general | solution.py:113
  4.5 2.7 %collective-permute-start = (f32[14,192]{1,0:T(8,128)S(1)}, f32[14,192]{1,0:T(8,128)S(1)}, u32[]{:S(2)}, u32[]{:S(2)}) collective-permute-start(f32[14,192]{1,0:T(8,128)S(1)} %reshape.355), channel_id=1, source_target_pairs={{0,1},{1,2},{2,3},{3,4},{4,5},{5,6},{6,7},{7,8},{8,9},{9,10},{10,1... | collective-permute-start | bytes 32264 | tf_op jit(solution)/shard_map/ppermute | solution.py:129
  7.2 0.9 collective-permute-done
  8.0 2.3 %collective-permute-start.2 = (f32[14,192]{1,0:T(8,128)S(1)}, f32[14,192]{1,0:T(8,128)S(1)}, u32[]{:S(2)}, u32[]{:S(2)}) collective-permute-start(f32[14,192]{1,0:T(8,128)S(1)} %collective-permute-done), channel_id=1, source_target_pairs={{0,1},{1,2},{2,3},{3,4},{4,5},{5,6},{6,7},{7,8},{8,9},{9,10},{10,1... | collective-permute-start | bytes 32264 | tf_op jit(solution)/shard_map/ppermute | solution.py:129
  10.6 0.9 collective-permute-start.3
  11.6 0.6 collective-permute-done.2
  12.1 1.4 %collective-permute-start.4 = (f32[14,192]{1,0:T(8,128)S(1)}, f32[14,192]{1,0:T(8,128)S(1)}, u32[]{:S(2)}, u32[]{:S(2)}) collective-permute-start(f32[14,192]{1,0:T(8,128)S(1)} %collective-permute-done.2), channel_id=1, source_target_pairs={{0,1},{1,2},{2,3},{3,4},{4,5},{5,6},{6,7},{7,8},{8,9},{9,10},{10,1... | collective-permute-start | bytes 32264 | tf_op jit(solution)/shard_map/ppermute | solution.py:129
  13.8 3.6 %collective-permute-start.5 = (f32[14,192]{1,0:T(8,128)S(1)}, f32[14,192]{1,0:T(8,128)S(1)}, u32[]{:S(2)}, u32[]{:S(2)}) collective-permute-start(f32[14,192]{1,0:T(8,128)S(1)} %collective-permute-done.3), channel_id=1, source_target_pairs={{0,15},{1,0},{2,1},{3,2},{4,3},{5,4},{6,5},{7,6},{8,7},{9,8},{10,9... | collective-permute-start | bytes 32264 | tf_op jit(solution)/shard_map/ppermute | solution.py:136
  17.4 0.6 collective-permute-done.4
  18.2 7.1 %collective-permute-start.18 = (f32[7,2,64,2]{3,2,1,0:T(8,128)S(1)}, f32[7,2,64,2]{3,2,1,0:T(8,128)S(1)}, u32[]{:S(2)}, u32[]{:S(2)}) collective-permute-start(f32[7,2,64,2]{3,2,1,0:T(8,128)S(1)} %get-tuple-element.36), channel_id=1, source_target_pairs={{1,0},{2,1},{3,2},{5,4},{6,5},{7,6},{9,8},{10,9},{11,10},{13,12},{... | collective-permute-start | bytes 21512 | tf_op jit(solution)/shard_map/ppermute | solution.py:30
  25.3 1.9 %collective-permute-start.19 = (f32[7,2,64,2]{3,2,1,0:T(8,128)S(1)}, f32[7,2,64,2]{3,2,1,0:T(8,128)S(1)}, u32[]{:S(2)}, u32[]{:S(2)}) collective-permute-start(f32[7,2,64,2]{3,2,1,0:T(8,128)S(1)} %get-tuple-element.35), channel_id=1, source_target_pairs={{0,1},{1,2},{2,3},{4,5},{5,6},{6,7},{8,9},{9,10},{10,11},{12,13},{... | collective-permute-start | bytes 21512 | tf_op jit(solution)/shard_map/ppermute | solution.py:30
  27.2 0.6 collective-permute-start.7
  27.8 1.2 collective-permute-start.8
  29.1 1.3 collective-permute-start.16
  30.5 1.5 %collective-permute-start.9 = (f32[14,192]{1,0:T(8,128)S(1)}, f32[14,192]{1,0:T(8,128)S(1)}, u32[]{:S(2)}, u32[]{:S(2)}) collective-permute-start(f32[14,192]{1,0:T(8,128)S(1)} %collective-permute-done.7), channel_id=1, source_target_pairs={{0,15},{1,0},{2,1},{3,2},{4,3},{5,4},{6,5},{7,6},{8,7},{9,8},{10,9... | collective-permute-start | bytes 32264 | tf_op jit(solution)/shard_map/ppermute | solution.py:136
  32.0 0.8 collective-permute-done.8
  32.8 2.5 %collective-permute-start.10 = (f32[14,192]{1,0:T(8,128)S(1)}, f32[14,192]{1,0:T(8,128)S(1)}, u32[]{:S(2)}, u32[]{:S(2)}) collective-permute-start(f32[14,192]{1,0:T(8,128)S(1)} %collective-permute-done.8), channel_id=1, source_target_pairs={{0,1},{1,2},{2,3},{3,4},{4,5},{5,6},{6,7},{7,8},{8,9},{9,10},{10,1... | collective-permute-start | bytes 32264 | tf_op jit(solution)/shard_map/ppermute | solution.py:129
  35.3 2.5 %collective-permute-start.11 = (f32[14,192]{1,0:T(8,128)S(1)}, f32[14,192]{1,0:T(8,128)S(1)}, u32[]{:S(2)}, u32[]{:S(2)}) collective-permute-start(f32[14,192]{1,0:T(8,128)S(1)} %collective-permute-done.9), channel_id=1, source_target_pairs={{0,15},{1,0},{2,1},{3,2},{4,3},{5,4},{6,5},{7,6},{8,7},{9,8},{10,9... | collective-permute-start | bytes 32264 | tf_op jit(solution)/shard_map/ppermute | solution.py:136
  37.8 0.6 collective-permute-start.12
  38.7 5.0 %collective-permute-start.13 = (f32[14,192]{1,0:T(8,128)S(1)}, f32[14,192]{1,0:T(8,128)S(1)}, u32[]{:S(2)}, u32[]{:S(2)}) collective-permute-start(f32[14,192]{1,0:T(8,128)S(1)} %collective-permute-done.11), channel_id=1, source_target_pairs={{0,15},{1,0},{2,1},{3,2},{4,3},{5,4},{6,5},{7,6},{8,7},{9,8},{10,9... | collective-permute-start | bytes 32264 | tf_op jit(solution)/shard_map/ppermute | solution.py:136
  43.7 0.5 dynamic_update_slice.96
  46.5 0.5 dynamic_update_slice.103
  47.0 0.5 dynamic_update_slice.104
  48.1 0.5 dynamic_update_slice.107
  48.6 0.5 dynamic_update_slice.108
  49.4 1.5 %collective-permute-start.17 = (f32[7,2,2,128]{3,2,1,0:T(2,128)S(1)}, f32[7,2,2,128]{3,2,1,0:T(2,128)S(1)}, u32[]{:S(2)}, u32[]{:S(2)}) collective-permute-start(f32[7,2,2,128]{3,2,1,0:T(2,128)S(1)} %get-tuple-element.37), channel_id=1, source_target_pairs={{0,4},{4,8},{8,12},{1,5},{5,9},{9,13},{2,6},{6,10},{10,14},{3,7},{... | collective-permute-start | bytes 43016 | tf_op jit(solution)/shard_map/ppermute | solution.py:30
  51.3 0.5 dynamic_update_slice.111
  51.8 1.8 %collective-permute-start.15 = (f32[14,3072]{1,0:T(8,128)S(1)}, f32[14,3072]{1,0:T(8,128)S(1)}, u32[]{:S(2)}, u32[]{:S(2)}) collective-permute-start(f32[14,3072]{1,0:T(8,128)S(1)} %dynamic_update_slice.111), channel_id=1, source_target_pairs={{0,16},{16,0},{1,17},{17,1},{2,18},{18,2},{3,19},{19,3},{4,20},{20... | collective-permute-start | bytes 516104 | tf_op jit(solution)/shard_map/ppermute | solution.py:21
  53.6 3.0 %collective-permute-done.15 = f32[14,3072]{1,0:T(8,128)S(1)} collective-permute-done((f32[14,3072]{1,0:T(8,128)S(1)}, f32[14,3072]{1,0:T(8,128)S(1)}, u32[]{:S(2)}, u32[]{:S(2)}) %collective-permute-start.15) | collective-permute-done | bytes 172064 | tf_op jit(solution)/shard_map/ppermute | solution.py:21
  56.6 1.5 %fusion.1 = f32[14,384]{1,0:T(8,128)S(1)} fusion(f32[14,3072]{1,0:T(8,128)S(1)} %collective-permute-done.15, s32[384]{0:T(512)S(1)} %pad_add_fusion), kind=kOutput, calls=%fused_computation.2 | convolution fusion | flops 199360512 | bytes 195072 | tf_op jit(solution)/shard_map/dot_general | solution.py:143
  58.7 0.9 multiply_add_fusion.2
  59.6 0.6 fusion.17
  60.5 1.0 fusion.5
  61.7 5.3 %collective-permute-start.21 = (f32[14,192]{1,0:T(8,128)S(1)}, f32[14,192]{1,0:T(8,128)S(1)}, u32[]{:S(2)}, u32[]{:S(2)}) collective-permute-start(f32[14,192]{1,0:T(8,128)S(1)} %reshape.359), channel_id=1, source_target_pairs={{0,15},{1,0},{2,1},{3,2},{4,3},{5,4},{6,5},{7,6},{8,7},{9,8},{10,9... | collective-permute-start | bytes 32264 | tf_op jit(solution)/shard_map/ppermute | solution.py:136
  67.1 0.6 collective-permute-done.20
  67.9 5.0 %collective-permute-start.23 = (f32[14,192]{1,0:T(8,128)S(1)}, f32[14,192]{1,0:T(8,128)S(1)}, u32[]{:S(2)}, u32[]{:S(2)}) collective-permute-start(f32[14,192]{1,0:T(8,128)S(1)} %collective-permute-done.21), channel_id=1, source_target_pairs={{0,15},{1,0},{2,1},{3,2},{4,3},{5,4},{6,5},{7,6},{8,7},{9,8},{10,9... | collective-permute-start | bytes 32264 | tf_op jit(solution)/shard_map/ppermute | solution.py:136
  72.9 0.7 collective-permute-done.22
  73.7 5.0 %collective-permute-start.25 = (f32[14,192]{1,0:T(8,128)S(1)}, f32[14,192]{1,0:T(8,128)S(1)}, u32[]{:S(2)}, u32[]{:S(2)}) collective-permute-start(f32[14,192]{1,0:T(8,128)S(1)} %collective-permute-done.23), channel_id=1, source_target_pairs={{0,15},{1,0},{2,1},{3,2},{4,3},{5,4},{6,5},{7,6},{8,7},{9,8},{10,9... | collective-permute-start | bytes 32264 | tf_op jit(solution)/shard_map/ppermute | solution.py:136
  78.7 0.6 collective-permute-done.24
  79.6 5.0 %collective-permute-start.27 = (f32[14,192]{1,0:T(8,128)S(1)}, f32[14,192]{1,0:T(8,128)S(1)}, u32[]{:S(2)}, u32[]{:S(2)}) collective-permute-start(f32[14,192]{1,0:T(8,128)S(1)} %collective-permute-done.25), channel_id=1, source_target_pairs={{0,15},{1,0},{2,1},{3,2},{4,3},{5,4},{6,5},{7,6},{8,7},{9,8},{10,9... | collective-permute-start | bytes 32264 | tf_op jit(solution)/shard_map/ppermute | solution.py:136
  84.6 0.6 collective-permute-done.26
  85.4 5.0 %collective-permute-start.29 = (f32[14,192]{1,0:T(8,128)S(1)}, f32[14,192]{1,0:T(8,128)S(1)}, u32[]{:S(2)}, u32[]{:S(2)}) collective-permute-start(f32[14,192]{1,0:T(8,128)S(1)} %collective-permute-done.27), channel_id=1, source_target_pairs={{0,15},{1,0},{2,1},{3,2},{4,3},{5,4},{6,5},{7,6},{8,7},{9,8},{10,9... | collective-permute-start | bytes 32264 | tf_op jit(solution)/shard_map/ppermute | solution.py:136
  90.5 0.6 collective-permute-done.28
  91.3 5.0 %collective-permute-start.31 = (f32[14,192]{1,0:T(8,128)S(1)}, f32[14,192]{1,0:T(8,128)S(1)}, u32[]{:S(2)}, u32[]{:S(2)}) collective-permute-start(f32[14,192]{1,0:T(8,128)S(1)} %collective-permute-done.29), channel_id=1, source_target_pairs={{0,15},{1,0},{2,1},{3,2},{4,3},{5,4},{6,5},{7,6},{8,7},{9,8},{10,9... | collective-permute-start | bytes 32264 | tf_op jit(solution)/shard_map/ppermute | solution.py:136
  96.3 0.6 collective-permute-done.30
  97.2 5.2 %collective-permute-start.33 = (f32[14,192]{1,0:T(8,128)S(1)}, f32[14,192]{1,0:T(8,128)S(1)}, u32[]{:S(2)}, u32[]{:S(2)}) collective-permute-start(f32[14,192]{1,0:T(8,128)S(1)} %collective-permute-done.31), channel_id=1, source_target_pairs={{0,15},{1,0},{2,1},{3,2},{4,3},{5,4},{6,5},{7,6},{8,7},{9,8},{10,9... | collective-permute-start | bytes 32264 | tf_op jit(solution)/shard_map/ppermute | solution.py:136
  102.9 0.5 dynamic_update_slice.112
  103.3 7.0 %collective-permute-start.38 = (f32[7,2,64,2]{3,2,1,0:T(8,128)S(1)}, f32[7,2,64,2]{3,2,1,0:T(8,128)S(1)}, u32[]{:S(2)}, u32[]{:S(2)}) collective-permute-start(f32[7,2,64,2]{3,2,1,0:T(8,128)S(1)} %get-tuple-element.24), channel_id=1, source_target_pairs={{1,0},{2,1},{3,2},{5,4},{6,5},{7,6},{9,8},{10,9},{11,10},{13,12},{... | collective-permute-start | bytes 21512 | tf_op jit(solution)/shard_map/ppermute | solution.py:30
  110.3 1.9 %collective-permute-start.39 = (f32[7,2,64,2]{3,2,1,0:T(8,128)S(1)}, f32[7,2,64,2]{3,2,1,0:T(8,128)}, u32[]{:S(2)}, u32[]{:S(2)}) collective-permute-start(f32[7,2,64,2]{3,2,1,0:T(8,128)S(1)} %get-tuple-element.23), channel_id=1, source_target_pairs={{0,1},{1,2},{2,3},{4,5},{5,6},{6,7},{8,9},{9,10},{10,11},{12,13},{... | collective-permute-start | bytes 21512 | tf_op jit(solution)/shard_map/ppermute | solution.py:30
  112.3 1.3 collective-permute-start.36
  115.8 0.5 dynamic_update_slice.119
  118.8 4.6 %collective-permute-start.37 = (f32[7,2,2,128]{3,2,1,0:T(2,128)S(1)}, f32[7,2,2,128]{3,2,1,0:T(2,128)}, u32[]{:S(2)}, u32[]{:S(2)}) collective-permute-start(f32[7,2,2,128]{3,2,1,0:T(2,128)S(1)} %get-tuple-element.25), channel_id=1, source_target_pairs={{0,4},{4,8},{8,12},{1,5},{5,9},{9,13},{2,6},{6,10},{10,14},{3,7},{... | collective-permute-start | bytes 43016 | tf_op jit(solution)/shard_map/ppermute | solution.py:30
  123.6 0.5 dynamic_update_slice.127
  124.0 1.8 %collective-permute-start.35 = (f32[14,3072]{1,0:T(8,128)S(1)}, f32[14,3072]{1,0:T(8,128)S(1)}, u32[]{:S(2)}, u32[]{:S(2)}) collective-permute-start(f32[14,3072]{1,0:T(8,128)S(1)} %dynamic_update_slice.127), channel_id=1, source_target_pairs={{0,16},{16,0},{1,17},{17,1},{2,18},{18,2},{3,19},{19,3},{4,20},{20... | collective-permute-start | bytes 516104 | tf_op jit(solution)/shard_map/ppermute | solution.py:21
  125.9 3.0 %collective-permute-done.35 = f32[14,3072]{1,0:T(8,128)S(1)} collective-permute-done((f32[14,3072]{1,0:T(8,128)S(1)}, f32[14,3072]{1,0:T(8,128)S(1)}, u32[]{:S(2)}, u32[]{:S(2)}) %collective-permute-start.35) | collective-permute-done | bytes 172064 | tf_op jit(solution)/shard_map/ppermute | solution.py:21
  128.9 1.5 %fusion = f32[14,384]{1,0:T(8,128)S(1)} fusion(f32[14,3072]{1,0:T(8,128)S(1)} %collective-permute-done.35, s32[384]{0:T(512)S(1)} %pad_add_fusion), kind=kOutput, calls=%fused_computation.1 | convolution fusion | flops 199360512 | bytes 195072 | tf_op jit(solution)/shard_map/dot_general | solution.py:143
  130.8 1.1 bitcast_select_fusion
  132.0 0.7 broadcast_select_fusion
  132.7 0.5 fusion.20
  133.3 0.9 multiply_add_fusion
  134.4 0.9 fusion.32
  (125 shorter events, 13.0 us)
Async XLA Ops:
  0.0 18.0 %copy-start = (f32[1,7,2,64,128]{4,3,2,1,0:T(8,128)S(1)}, f32[1,7,2,64,128]{4,3,2,1,0:T(8,128)}, u32[]{:S(2)}) copy-start(f32[1,7,2,64,128]{4,3,2,1,0:T(8,128)} %param.5) | copy-start | bytes 1376260
  0.0 4.3 %copy-start.2 = (f32[1,1,1,192]{3,2,1,0:T(1,128)S(1)}, f32[1,1,1,192]{3,2,1,0:T(1,128)}, u32[]{:S(2)}) copy-start(f32[1,1,1,192]{3,2,1,0:T(1,128)} %param.9) | copy-start | bytes 2308
  4.5 3.5 %collective-permute-start = (f32[14,192]{1,0:T(8,128)S(1)}, f32[14,192]{1,0:T(8,128)S(1)}, u32[]{:S(2)}, u32[]{:S(2)}) collective-permute-start(f32[14,192]{1,0:T(8,128)S(1)} %reshape.355), channel_id=1, source_target_pairs={{0,1},{1,2},{2,3},{3,4},{4,5},{5,6},{6,7},{7,8},{8,9},{9,10},{10,1... | collective-permute-start | bytes 32264 | tf_op jit(solution)/shard_map/ppermute | solution.py:129
  7.2 3.5 %collective-permute-start.1 = (f32[14,192]{1,0:T(8,128)S(1)}, f32[14,192]{1,0:T(8,128)S(1)}, u32[]{:S(2)}, u32[]{:S(2)}) collective-permute-start(f32[14,192]{1,0:T(8,128)S(1)} %reshape.355), channel_id=1, source_target_pairs={{0,15},{1,0},{2,1},{3,2},{4,3},{5,4},{6,5},{7,6},{8,7},{9,8},{10,9... | collective-permute-start | bytes 32264 | tf_op jit(solution)/shard_map/ppermute | solution.py:136
  8.0 4.1 %collective-permute-start.2 = (f32[14,192]{1,0:T(8,128)S(1)}, f32[14,192]{1,0:T(8,128)S(1)}, u32[]{:S(2)}, u32[]{:S(2)}) collective-permute-start(f32[14,192]{1,0:T(8,128)S(1)} %collective-permute-done), channel_id=1, source_target_pairs={{0,1},{1,2},{2,3},{3,4},{4,5},{5,6},{6,7},{7,8},{8,9},{9,10},{10,1... | collective-permute-start | bytes 32264 | tf_op jit(solution)/shard_map/ppermute | solution.py:129
  10.6 3.2 %collective-permute-start.3 = (f32[14,192]{1,0:T(8,128)S(1)}, f32[14,192]{1,0:T(8,128)S(1)}, u32[]{:S(2)}, u32[]{:S(2)}) collective-permute-start(f32[14,192]{1,0:T(8,128)S(1)} %collective-permute-done.1), channel_id=1, source_target_pairs={{0,15},{1,0},{2,1},{3,2},{4,3},{5,4},{6,5},{7,6},{8,7},{9,8},{10,9... | collective-permute-start | bytes 32264 | tf_op jit(solution)/shard_map/ppermute | solution.py:136
  12.1 5.9 %collective-permute-start.4 = (f32[14,192]{1,0:T(8,128)S(1)}, f32[14,192]{1,0:T(8,128)S(1)}, u32[]{:S(2)}, u32[]{:S(2)}) collective-permute-start(f32[14,192]{1,0:T(8,128)S(1)} %collective-permute-done.2), channel_id=1, source_target_pairs={{0,1},{1,2},{2,3},{3,4},{4,5},{5,6},{6,7},{7,8},{8,9},{9,10},{10,1... | collective-permute-start | bytes 32264 | tf_op jit(solution)/shard_map/ppermute | solution.py:129
  13.8 13.4 %collective-permute-start.5 = (f32[14,192]{1,0:T(8,128)S(1)}, f32[14,192]{1,0:T(8,128)S(1)}, u32[]{:S(2)}, u32[]{:S(2)}) collective-permute-start(f32[14,192]{1,0:T(8,128)S(1)} %collective-permute-done.3), channel_id=1, source_target_pairs={{0,15},{1,0},{2,1},{3,2},{4,3},{5,4},{6,5},{7,6},{8,7},{9,8},{10,9... | collective-permute-start | bytes 32264 | tf_op jit(solution)/shard_map/ppermute | solution.py:136
  18.0 9.8 %collective-permute-start.6 = (f32[14,192]{1,0:T(8,128)S(1)}, f32[14,192]{1,0:T(8,128)S(1)}, u32[]{:S(2)}, u32[]{:S(2)}) collective-permute-start(f32[14,192]{1,0:T(8,128)S(1)} %collective-permute-done.4), channel_id=1, source_target_pairs={{0,1},{1,2},{2,3},{3,4},{4,5},{5,6},{6,7},{7,8},{8,9},{9,10},{10,1... | collective-permute-start | bytes 32264 | tf_op jit(solution)/shard_map/ppermute | solution.py:129
  18.2 20.3 %copy-start.1 = (s32[1,1,1,768]{3,2,1,0:T(1,128)S(1)}, s32[1,1,1,768]{3,2,1,0:T(1,128)}, u32[]{:S(2)}) copy-start(s32[1,1,1,768]{3,2,1,0:T(1,128)} %param.6) | copy-start | bytes 9220
  18.2 40.3 %collective-permute-start.18 = (f32[7,2,64,2]{3,2,1,0:T(8,128)S(1)}, f32[7,2,64,2]{3,2,1,0:T(8,128)S(1)}, u32[]{:S(2)}, u32[]{:S(2)}) collective-permute-start(f32[7,2,64,2]{3,2,1,0:T(8,128)S(1)} %get-tuple-element.36), channel_id=1, source_target_pairs={{1,0},{2,1},{3,2},{5,4},{6,5},{7,6},{9,8},{10,9},{11,10},{13,12},{... | collective-permute-start | bytes 21512 | tf_op jit(solution)/shard_map/ppermute | solution.py:30
  25.3 33.2 %collective-permute-start.19 = (f32[7,2,64,2]{3,2,1,0:T(8,128)S(1)}, f32[7,2,64,2]{3,2,1,0:T(8,128)S(1)}, u32[]{:S(2)}, u32[]{:S(2)}) collective-permute-start(f32[7,2,64,2]{3,2,1,0:T(8,128)S(1)} %get-tuple-element.35), channel_id=1, source_target_pairs={{0,1},{1,2},{2,3},{4,5},{5,6},{6,7},{8,9},{9,10},{10,11},{12,13},{... | collective-permute-start | bytes 21512 | tf_op jit(solution)/shard_map/ppermute | solution.py:30
  27.2 3.2 %collective-permute-start.7 = (f32[14,192]{1,0:T(8,128)S(1)}, f32[14,192]{1,0:T(8,128)S(1)}, u32[]{:S(2)}, u32[]{:S(2)}) collective-permute-start(f32[14,192]{1,0:T(8,128)S(1)} %collective-permute-done.5), channel_id=1, source_target_pairs={{0,15},{1,0},{2,1},{3,2},{4,3},{5,4},{6,5},{7,6},{8,7},{9,8},{10,9... | collective-permute-start | bytes 32264 | tf_op jit(solution)/shard_map/ppermute | solution.py:136
  27.8 5.0 %collective-permute-start.8 = (f32[14,192]{1,0:T(8,128)S(1)}, f32[14,192]{1,0:T(8,128)S(1)}, u32[]{:S(2)}, u32[]{:S(2)}) collective-permute-start(f32[14,192]{1,0:T(8,128)S(1)} %collective-permute-done.6), channel_id=1, source_target_pairs={{0,1},{1,2},{2,3},{3,4},{4,5},{5,6},{6,7},{7,8},{8,9},{9,10},{10,1... | collective-permute-start | bytes 32264 | tf_op jit(solution)/shard_map/ppermute | solution.py:129
  29.1 29.6 %collective-permute-start.16 = (f32[7,2,2,128]{3,2,1,0:T(2,128)S(1)}, f32[7,2,2,128]{3,2,1,0:T(2,128)S(1)}, u32[]{:S(2)}, u32[]{:S(2)}) collective-permute-start(f32[7,2,2,128]{3,2,1,0:T(2,128)S(1)} %get-tuple-element.38), channel_id=1, source_target_pairs={{4,0},{8,4},{12,8},{5,1},{9,5},{13,9},{6,2},{10,6},{14,10},{7,3},{... | collective-permute-start | bytes 43016 | tf_op jit(solution)/shard_map/ppermute | solution.py:30
  30.5 4.9 %collective-permute-start.9 = (f32[14,192]{1,0:T(8,128)S(1)}, f32[14,192]{1,0:T(8,128)S(1)}, u32[]{:S(2)}, u32[]{:S(2)}) collective-permute-start(f32[14,192]{1,0:T(8,128)S(1)} %collective-permute-done.7), channel_id=1, source_target_pairs={{0,15},{1,0},{2,1},{3,2},{4,3},{5,4},{6,5},{7,6},{8,7},{9,8},{10,9... | collective-permute-start | bytes 32264 | tf_op jit(solution)/shard_map/ppermute | solution.py:136
  32.8 5.0 %collective-permute-start.10 = (f32[14,192]{1,0:T(8,128)S(1)}, f32[14,192]{1,0:T(8,128)S(1)}, u32[]{:S(2)}, u32[]{:S(2)}) collective-permute-start(f32[14,192]{1,0:T(8,128)S(1)} %collective-permute-done.8), channel_id=1, source_target_pairs={{0,1},{1,2},{2,3},{3,4},{4,5},{5,6},{6,7},{7,8},{8,9},{9,10},{10,1... | collective-permute-start | bytes 32264 | tf_op jit(solution)/shard_map/ppermute | solution.py:129
  35.3 3.3 %collective-permute-start.11 = (f32[14,192]{1,0:T(8,128)S(1)}, f32[14,192]{1,0:T(8,128)S(1)}, u32[]{:S(2)}, u32[]{:S(2)}) collective-permute-start(f32[14,192]{1,0:T(8,128)S(1)} %collective-permute-done.9), channel_id=1, source_target_pairs={{0,15},{1,0},{2,1},{3,2},{4,3},{5,4},{6,5},{7,6},{8,7},{9,8},{10,9... | collective-permute-start | bytes 32264 | tf_op jit(solution)/shard_map/ppermute | solution.py:136
  37.8 5.9 %collective-permute-start.12 = (f32[14,192]{1,0:T(8,128)S(1)}, f32[14,192]{1,0:T(8,128)S(1)}, u32[]{:S(2)}, u32[]{:S(2)}) collective-permute-start(f32[14,192]{1,0:T(8,128)S(1)} %collective-permute-done.10), channel_id=1, source_target_pairs={{0,1},{1,2},{2,3},{3,4},{4,5},{5,6},{6,7},{7,8},{8,9},{9,10},{10,1... | collective-permute-start | bytes 32264 | tf_op jit(solution)/shard_map/ppermute | solution.py:129
  38.7 10.8 %collective-permute-start.13 = (f32[14,192]{1,0:T(8,128)S(1)}, f32[14,192]{1,0:T(8,128)S(1)}, u32[]{:S(2)}, u32[]{:S(2)}) collective-permute-start(f32[14,192]{1,0:T(8,128)S(1)} %collective-permute-done.11), channel_id=1, source_target_pairs={{0,15},{1,0},{2,1},{3,2},{4,3},{5,4},{6,5},{7,6},{8,7},{9,8},{10,9... | collective-permute-start | bytes 32264 | tf_op jit(solution)/shard_map/ppermute | solution.py:136
  43.7 7.6 %collective-permute-start.14 = (f32[14,192]{1,0:T(8,128)S(1)}, f32[14,192]{1,0:T(8,128)S(1)}, u32[]{:S(2)}, u32[]{:S(2)}) collective-permute-start(f32[14,192]{1,0:T(8,128)S(1)} %collective-permute-done.12), channel_id=1, source_target_pairs={{0,1},{1,2},{2,3},{3,4},{4,5},{5,6},{6,7},{7,8},{8,9},{9,10},{10,1... | collective-permute-start | bytes 32264 | tf_op jit(solution)/shard_map/ppermute | solution.py:129
  49.4 9.2 %collective-permute-start.17 = (f32[7,2,2,128]{3,2,1,0:T(2,128)S(1)}, f32[7,2,2,128]{3,2,1,0:T(2,128)S(1)}, u32[]{:S(2)}, u32[]{:S(2)}) collective-permute-start(f32[7,2,2,128]{3,2,1,0:T(2,128)S(1)} %get-tuple-element.37), channel_id=1, source_target_pairs={{0,4},{4,8},{8,12},{1,5},{5,9},{9,13},{2,6},{6,10},{10,14},{3,7},{... | collective-permute-start | bytes 43016 | tf_op jit(solution)/shard_map/ppermute | solution.py:30
  51.8 4.9 %collective-permute-start.15 = (f32[14,3072]{1,0:T(8,128)S(1)}, f32[14,3072]{1,0:T(8,128)S(1)}, u32[]{:S(2)}, u32[]{:S(2)}) collective-permute-start(f32[14,3072]{1,0:T(8,128)S(1)} %dynamic_update_slice.111), channel_id=1, source_target_pairs={{0,16},{16,0},{1,17},{17,1},{2,18},{18,2},{3,19},{19,3},{4,20},{20... | collective-permute-start | bytes 516104 | tf_op jit(solution)/shard_map/ppermute | solution.py:21
  61.7 6.0 %collective-permute-start.20 = (f32[14,192]{1,0:T(8,128)S(1)}, f32[14,192]{1,0:T(8,128)S(1)}, u32[]{:S(2)}, u32[]{:S(2)}) collective-permute-start(f32[14,192]{1,0:T(8,128)S(1)} %reshape.359), channel_id=1, source_target_pairs={{0,1},{1,2},{2,3},{3,4},{4,5},{5,6},{6,7},{7,8},{8,9},{9,10},{10,1... | collective-permute-start | bytes 32264 | tf_op jit(solution)/shard_map/ppermute | solution.py:129
  61.7 6.2 %collective-permute-start.21 = (f32[14,192]{1,0:T(8,128)S(1)}, f32[14,192]{1,0:T(8,128)S(1)}, u32[]{:S(2)}, u32[]{:S(2)}) collective-permute-start(f32[14,192]{1,0:T(8,128)S(1)} %reshape.359), channel_id=1, source_target_pairs={{0,15},{1,0},{2,1},{3,2},{4,3},{5,4},{6,5},{7,6},{8,7},{9,8},{10,9... | collective-permute-start | bytes 32264 | tf_op jit(solution)/shard_map/ppermute | solution.py:136
  67.7 5.9 %collective-permute-start.22 = (f32[14,192]{1,0:T(8,128)S(1)}, f32[14,192]{1,0:T(8,128)S(1)}, u32[]{:S(2)}, u32[]{:S(2)}) collective-permute-start(f32[14,192]{1,0:T(8,128)S(1)} %collective-permute-done.20), channel_id=1, source_target_pairs={{0,1},{1,2},{2,3},{3,4},{4,5},{5,6},{6,7},{7,8},{8,9},{9,10},{10,1... | collective-permute-start | bytes 32264 | tf_op jit(solution)/shard_map/ppermute | solution.py:129
  67.9 5.8 %collective-permute-start.23 = (f32[14,192]{1,0:T(8,128)S(1)}, f32[14,192]{1,0:T(8,128)S(1)}, u32[]{:S(2)}, u32[]{:S(2)}) collective-permute-start(f32[14,192]{1,0:T(8,128)S(1)} %collective-permute-done.21), channel_id=1, source_target_pairs={{0,15},{1,0},{2,1},{3,2},{4,3},{5,4},{6,5},{7,6},{8,7},{9,8},{10,9... | collective-permute-start | bytes 32264 | tf_op jit(solution)/shard_map/ppermute | solution.py:136
  73.5 5.9 %collective-permute-start.24 = (f32[14,192]{1,0:T(8,128)S(1)}, f32[14,192]{1,0:T(8,128)S(1)}, u32[]{:S(2)}, u32[]{:S(2)}) collective-permute-start(f32[14,192]{1,0:T(8,128)S(1)} %collective-permute-done.22), channel_id=1, source_target_pairs={{0,1},{1,2},{2,3},{3,4},{4,5},{5,6},{6,7},{7,8},{8,9},{9,10},{10,1... | collective-permute-start | bytes 32264 | tf_op jit(solution)/shard_map/ppermute | solution.py:129
  73.7 5.9 %collective-permute-start.25 = (f32[14,192]{1,0:T(8,128)S(1)}, f32[14,192]{1,0:T(8,128)S(1)}, u32[]{:S(2)}, u32[]{:S(2)}) collective-permute-start(f32[14,192]{1,0:T(8,128)S(1)} %collective-permute-done.23), channel_id=1, source_target_pairs={{0,15},{1,0},{2,1},{3,2},{4,3},{5,4},{6,5},{7,6},{8,7},{9,8},{10,9... | collective-permute-start | bytes 32264 | tf_op jit(solution)/shard_map/ppermute | solution.py:136
  79.4 5.9 %collective-permute-start.26 = (f32[14,192]{1,0:T(8,128)S(1)}, f32[14,192]{1,0:T(8,128)S(1)}, u32[]{:S(2)}, u32[]{:S(2)}) collective-permute-start(f32[14,192]{1,0:T(8,128)S(1)} %collective-permute-done.24), channel_id=1, source_target_pairs={{0,1},{1,2},{2,3},{3,4},{4,5},{5,6},{6,7},{7,8},{8,9},{9,10},{10,1... | collective-permute-start | bytes 32264 | tf_op jit(solution)/shard_map/ppermute | solution.py:129
  79.6 5.9 %collective-permute-start.27 = (f32[14,192]{1,0:T(8,128)S(1)}, f32[14,192]{1,0:T(8,128)S(1)}, u32[]{:S(2)}, u32[]{:S(2)}) collective-permute-start(f32[14,192]{1,0:T(8,128)S(1)} %collective-permute-done.25), channel_id=1, source_target_pairs={{0,15},{1,0},{2,1},{3,2},{4,3},{5,4},{6,5},{7,6},{8,7},{9,8},{10,9... | collective-permute-start | bytes 32264 | tf_op jit(solution)/shard_map/ppermute | solution.py:136
  85.3 5.9 %collective-permute-start.28 = (f32[14,192]{1,0:T(8,128)S(1)}, f32[14,192]{1,0:T(8,128)S(1)}, u32[]{:S(2)}, u32[]{:S(2)}) collective-permute-start(f32[14,192]{1,0:T(8,128)S(1)} %collective-permute-done.26), channel_id=1, source_target_pairs={{0,1},{1,2},{2,3},{3,4},{4,5},{5,6},{6,7},{7,8},{8,9},{9,10},{10,1... | collective-permute-start | bytes 32264 | tf_op jit(solution)/shard_map/ppermute | solution.py:129
  85.4 5.9 %collective-permute-start.29 = (f32[14,192]{1,0:T(8,128)S(1)}, f32[14,192]{1,0:T(8,128)S(1)}, u32[]{:S(2)}, u32[]{:S(2)}) collective-permute-start(f32[14,192]{1,0:T(8,128)S(1)} %collective-permute-done.27), channel_id=1, source_target_pairs={{0,15},{1,0},{2,1},{3,2},{4,3},{5,4},{6,5},{7,6},{8,7},{9,8},{10,9... | collective-permute-start | bytes 32264 | tf_op jit(solution)/shard_map/ppermute | solution.py:136
  91.1 5.9 %collective-permute-start.30 = (f32[14,192]{1,0:T(8,128)S(1)}, f32[14,192]{1,0:T(8,128)S(1)}, u32[]{:S(2)}, u32[]{:S(2)}) collective-permute-start(f32[14,192]{1,0:T(8,128)S(1)} %collective-permute-done.28), channel_id=1, source_target_pairs={{0,1},{1,2},{2,3},{3,4},{4,5},{5,6},{6,7},{7,8},{8,9},{9,10},{10,1... | collective-permute-start | bytes 32264 | tf_op jit(solution)/shard_map/ppermute | solution.py:129
  91.3 5.9 %collective-permute-start.31 = (f32[14,192]{1,0:T(8,128)S(1)}, f32[14,192]{1,0:T(8,128)S(1)}, u32[]{:S(2)}, u32[]{:S(2)}) collective-permute-start(f32[14,192]{1,0:T(8,128)S(1)} %collective-permute-done.29), channel_id=1, source_target_pairs={{0,15},{1,0},{2,1},{3,2},{4,3},{5,4},{6,5},{7,6},{8,7},{9,8},{10,9... | collective-permute-start | bytes 32264 | tf_op jit(solution)/shard_map/ppermute | solution.py:136
  97.0 5.9 %collective-permute-start.32 = (f32[14,192]{1,0:T(8,128)S(1)}, f32[14,192]{1,0:T(8,128)S(1)}, u32[]{:S(2)}, u32[]{:S(2)}) collective-permute-start(f32[14,192]{1,0:T(8,128)S(1)} %collective-permute-done.30), channel_id=1, source_target_pairs={{0,1},{1,2},{2,3},{3,4},{4,5},{5,6},{6,7},{7,8},{8,9},{9,10},{10,1... | collective-permute-start | bytes 32264 | tf_op jit(solution)/shard_map/ppermute | solution.py:129
  97.2 21.6 %collective-permute-start.33 = (f32[14,192]{1,0:T(8,128)S(1)}, f32[14,192]{1,0:T(8,128)S(1)}, u32[]{:S(2)}, u32[]{:S(2)}) collective-permute-start(f32[14,192]{1,0:T(8,128)S(1)} %collective-permute-done.31), channel_id=1, source_target_pairs={{0,15},{1,0},{2,1},{3,2},{4,3},{5,4},{6,5},{7,6},{8,7},{9,8},{10,9... | collective-permute-start | bytes 32264 | tf_op jit(solution)/shard_map/ppermute | solution.py:136
  102.8 20.7 %collective-permute-start.34 = (f32[14,192]{1,0:T(8,128)S(1)}, f32[14,192]{1,0:T(8,128)S(1)}, u32[]{:S(2)}, u32[]{:S(2)}) collective-permute-start(f32[14,192]{1,0:T(8,128)S(1)} %collective-permute-done.32), channel_id=1, source_target_pairs={{0,1},{1,2},{2,3},{3,4},{4,5},{5,6},{6,7},{7,8},{8,9},{9,10},{10,1... | collective-permute-start | bytes 32264 | tf_op jit(solution)/shard_map/ppermute | solution.py:129
  103.3 27.4 %collective-permute-start.38 = (f32[7,2,64,2]{3,2,1,0:T(8,128)S(1)}, f32[7,2,64,2]{3,2,1,0:T(8,128)S(1)}, u32[]{:S(2)}, u32[]{:S(2)}) collective-permute-start(f32[7,2,64,2]{3,2,1,0:T(8,128)S(1)} %get-tuple-element.24), channel_id=1, source_target_pairs={{1,0},{2,1},{3,2},{5,4},{6,5},{7,6},{9,8},{10,9},{11,10},{13,12},{... | collective-permute-start | bytes 21512 | tf_op jit(solution)/shard_map/ppermute | solution.py:30
  110.3 20.4 %collective-permute-start.39 = (f32[7,2,64,2]{3,2,1,0:T(8,128)S(1)}, f32[7,2,64,2]{3,2,1,0:T(8,128)}, u32[]{:S(2)}, u32[]{:S(2)}) collective-permute-start(f32[7,2,64,2]{3,2,1,0:T(8,128)S(1)} %get-tuple-element.23), channel_id=1, source_target_pairs={{0,1},{1,2},{2,3},{4,5},{5,6},{6,7},{8,9},{9,10},{10,11},{12,13},{... | collective-permute-start | bytes 21512 | tf_op jit(solution)/shard_map/ppermute | solution.py:30
  112.3 19.7 %collective-permute-start.36 = (f32[7,2,2,128]{3,2,1,0:T(2,128)S(1)}, f32[7,2,2,128]{3,2,1,0:T(2,128)}, u32[]{:S(2)}, u32[]{:S(2)}) collective-permute-start(f32[7,2,2,128]{3,2,1,0:T(2,128)S(1)} %get-tuple-element.26), channel_id=1, source_target_pairs={{4,0},{8,4},{12,8},{5,1},{9,5},{13,9},{6,2},{10,6},{14,10},{7,3},{... | collective-permute-start | bytes 43016 | tf_op jit(solution)/shard_map/ppermute | solution.py:30
  118.8 13.2 %collective-permute-start.37 = (f32[7,2,2,128]{3,2,1,0:T(2,128)S(1)}, f32[7,2,2,128]{3,2,1,0:T(2,128)}, u32[]{:S(2)}, u32[]{:S(2)}) collective-permute-start(f32[7,2,2,128]{3,2,1,0:T(2,128)S(1)} %get-tuple-element.25), channel_id=1, source_target_pairs={{0,4},{4,8},{8,12},{1,5},{5,9},{9,13},{2,6},{6,10},{10,14},{3,7},{... | collective-permute-start | bytes 43016 | tf_op jit(solution)/shard_map/ppermute | solution.py:30
  124.0 4.9 %collective-permute-start.35 = (f32[14,3072]{1,0:T(8,128)S(1)}, f32[14,3072]{1,0:T(8,128)S(1)}, u32[]{:S(2)}, u32[]{:S(2)}) collective-permute-start(f32[14,3072]{1,0:T(8,128)S(1)} %dynamic_update_slice.127), channel_id=1, source_target_pairs={{0,16},{16,0},{1,17},{17,1},{2,18},{18,2},{3,19},{19,3},{4,20},{20... | collective-permute-start | bytes 516104 | tf_op jit(solution)/shard_map/ppermute | solution.py:21
